TPU v7x, 256 devices: a whole 4x4x8 slice. The times are simulated.
256 devices in a mesh: seq: 32 (over x, z), tp: 8 (over y, core).
Axes of the slice: x: 4, y: 4, z: 8, core: 2. Of those that a mesh axis runs over, the one named last changes fastest.
Arguments:
- tokens: bfloat16 [32768, 2048], P('seq', 'tp'), may hold values from -6 to 6
- w_inner: bfloat16 [2048, 2, 4096], P('seq', None, 'tp'), may hold values from -0.125 to 0.125
- w_states: bfloat16 [2048, 256], P('seq'), may hold values from -0.125 to 0.125
- w_step: bfloat16 [2048, 64], P('seq', 'tp'), may hold values from -0.125 to 0.125
- conv_inner: float32 [4, 4096], P(None, 'tp'), may hold values from -3 to 3
- conv_states: float32 [4, 256], replicated, may hold values from -3 to 3
- decay_rate: float32 [64], P('tp'), may hold values from 0 to 1, as said below
- step_bias: float32 [64], P('tp'), may hold values from -1 to 0.5
- skip_gain: float32 [64], P('tp'), may hold values from 0.5 to 1.5
- norm_gain: float32 [4096], P('tp'), may hold values from 0.5 to 1.5
- w_output: bfloat16 [4096, 2048], P('tp', 'seq'), may hold values from -0.09375 to 0.09375
- block_owner: int32 [128], replicated, may hold values from 0 to 19, as said below
- lengths: int32 [20], replicated, may hold values from 1 to 16384, as said below
Outputs:
- mixed: bfloat16 [32768, 2048], P('seq', 'tp')
Inputs may be any that keep to these rules, and one draw needn't show every extreme that they name: `block_owner`: each prompt's blocks are consecutive, prompt r has ceil(lengths[r] / 256) of them, and the prompts follow one another in an order drawn afresh; one prompt has 64 blocks and is neither the first nor the last in that order. `lengths`: one prompt has exactly 16384 tokens. `decay_rate`: Positive.
All inputs are finite; a program needn't handle non-finite values.
Results may differ from a plain program's by a relative error of at most 0.0075.
Values may be sent and summed in bfloat16 or wider, within the bound.
No kernel may reach another device: no remote copies, remote signals or barrier semaphores. Data moves between devices by JAX's collectives and lax.ppermute only.
A program may use at most 64 MiB of HBM per device.

v0:
```python
import jax
import jax.numpy as jnp
from jax import lax
from jax.sharding import Mesh
from jax.sharding import PartitionSpec as P

BLOCK = 256
LONGEST = 64
SEQ = ("sx", "sz")
SEQ_INNER = 8


def passed_along(value, axis, by):
    count = lax.axis_size(axis)
    pairs = [(i, i + by) for i in range(count) if 0 <= i + by < count]
    return lax.ppermute(value, axis, pairs)


def convolve(values, edge_rows, weights, in_block, carry_on):
    lag_rows = weights.shape[0] - 1
    row_total = values.shape[0]
    widened = jnp.concatenate([edge_rows, values], axis=0).astype(jnp.float32)
    total = jnp.zeros(values.shape, jnp.float32)
    for offset in range(weights.shape[0]):
        shifted = widened[lag_rows - offset : lag_rows - offset + row_total]
        keeping = (in_block >= offset) | carry_on
        total = total + jnp.where(keeping[:, None], shifted, 0.0) * weights[offset]
    return jax.nn.silu(total).astype(jnp.bfloat16)


def on_device(
    tokens,
    w_inner,
    w_states,
    w_step,
    conv_inner,
    conv_states,
    decay_rate,
    step_bias,
    skip_gain,
    norm_gain,
    w_output,
    block_owner,
    lengths,
):
    row_count = tokens.shape[0]
    local_blocks = row_count // BLOCK
    total_blocks = block_owner.shape[0]
    heads_here = w_step.shape[1]
    inner_here = w_inner.shape[2]
    state_size = w_states.shape[1] // 2
    head_size = inner_here // heads_here
    lag_rows = conv_inner.shape[0] - 1
    block_ids = jnp.arange(total_blocks, dtype=jnp.int32)
    same_owner = block_owner[:, None] == block_owner[None, :]
    first_block = jnp.min(jnp.where(same_owner, block_ids[None, :], total_blocks), axis=1)
    starting = (first_block == block_ids).astype(jnp.int32)
    request_ids = jnp.arange(lengths.shape[0], dtype=jnp.int32)
    own_length = jnp.sum(
        jnp.where(block_owner[:, None] == request_ids[None, :], lengths[None, :], 0), axis=1
    )
    valid_rows = jnp.clip(own_length - (block_ids - first_block) * BLOCK, 0, BLOCK)
    seq_index = lax.axis_index(SEQ)
    local_start = lax.dynamic_slice_in_dim(starting, seq_index * local_blocks, local_blocks)
    local_valid = lax.dynamic_slice_in_dim(valid_rows, seq_index * local_blocks, local_blocks)
    in_block = jnp.arange(row_count, dtype=jnp.int32) % BLOCK
    carry_on = jnp.repeat(local_start == 0, BLOCK)
    whole = lax.all_gather(tokens, "tp", axis=1, tiled=True)
    local_rows = w_inner.shape[0]
    joined = jnp.concatenate(
        [w_inner.reshape(local_rows, 2 * inner_here), w_states, w_step], axis=1
    )
    weights = lax.all_gather(
        lax.all_gather(joined, "sz", axis=0, tiled=True), "sx", axis=0, tiled=True
    )
    all_sum = jnp.dot(whole, weights, preferred_element_type=jnp.float32)
    projected = all_sum.astype(jnp.bfloat16)
    gate_in = projected[:, :inner_here]
    x_in = projected[:, inner_here : 2 * inner_here]
    bc_in = projected[:, 2 * inner_here : 2 * inner_here + 2 * state_size]
    step_raw = projected[:, 2 * inner_here + 2 * state_size :]
    edge_inner, edge_states = passed_along(
        (x_in[row_count - lag_rows :], bc_in[row_count - lag_rows :]), SEQ, 1
    )
    x_conv = convolve(x_in, edge_inner, conv_inner, in_block, carry_on)
    bc_conv = convolve(bc_in, edge_states, conv_states, in_block, carry_on)
    step_size = jax.nn.softplus(step_raw.astype(jnp.float32) + step_bias)
    log_decay = -decay_rate * step_size
    x_heads = x_conv.reshape(local_blocks, BLOCK, heads_here, head_size)
    b_rows = bc_conv[:, :state_size].reshape(local_blocks, BLOCK, state_size)
    c_rows = bc_conv[:, state_size:].reshape(local_blocks, BLOCK, state_size)
    step_blocks = step_size.reshape(local_blocks, BLOCK, heads_here)
    cumulative = jnp.cumsum(log_decay.reshape(local_blocks, BLOCK, heads_here), axis=1)
    causal = jnp.arange(BLOCK)[:, None] >= jnp.arange(BLOCK)[None, :]
    spread = cumulative[:, :, None, :] - cumulative[:, None, :, :]
    decays = jnp.exp(jnp.where(causal[None, :, :, None], spread, -jnp.inf))
    intersection = jnp.einsum("cin,cjn->cij", c_rows, b_rows, preferred_element_type=jnp.float32)
    mixing = (decays * intersection[:, :, :, None] * step_blocks[:, None, :, :]).astype(
        jnp.bfloat16
    )
    y_inner = jnp.einsum("cijh,cjhp->cihp", mixing, x_heads, preferred_element_type=jnp.float32)
    final_log = cumulative[:, -1, :]
    tail_weight = jnp.exp(final_log[:, None, :] - cumulative) * step_blocks
    weighted_b = (tail_weight[:, :, :, None] * b_rows.astype(jnp.float32)[:, :, None, :]).astype(
        jnp.bfloat16
    )
    fresh = jnp.einsum("cjhn,cjhp->chnp", weighted_b, x_heads, preferred_element_type=jnp.float32)
    keep_flag = jnp.where(local_start == 1, 0.0, 1.0).astype(jnp.float32)
    block_gain_each = jnp.exp(final_log) * keep_flag[:, None]

    def fold_block(carry, item):
        gain_now, fresh_now = item
        return ((carry[0] * gain_now, gain_now[:, None, None] * carry[1] + fresh_now), None)

    zero_state = jnp.zeros((heads_here, state_size, head_size), jnp.float32)
    unit_gain = jnp.ones((heads_here,), jnp.float32)
    (block_gain, block_state), _ = lax.scan(
        fold_block, (unit_gain, zero_state), (block_gain_each, fresh)
    )

    def packed(gain, state):
        rows = jnp.broadcast_to(gain[:, None, None], (heads_here, 1, head_size))
        return jnp.concatenate([state, rows], axis=1)

    prefix = passed_along(packed(block_gain, block_state), SEQ, 1)
    needed = min(-(-(LONGEST - 1) // local_blocks), lax.axis_size(SEQ) - 1)
    reach = 1
    while reach < needed:
        earlier = passed_along(prefix, SEQ, reach)
        gain_now = prefix[:, state_size:, :1]
        prefix = jnp.concatenate(
            [
                gain_now * earlier[:, :state_size] + prefix[:, :state_size],
                gain_now * earlier[:, state_size:],
            ],
            axis=1,
        )
        reach *= 2
    entering = prefix[:, :state_size]

    def pass_block(previous, item):
        log_now, keep_now, fresh_now = item
        incoming = previous * keep_now
        return (jnp.exp(log_now)[:, None, None] * incoming + fresh_now, incoming)

    _, incoming_all = lax.scan(pass_block, entering, (final_log, keep_flag, fresh))
    incoming_half = incoming_all.astype(jnp.bfloat16)
    y_carry = jnp.exp(cumulative)[:, :, :, None] * jnp.einsum(
        "cin,chnp->cihp", c_rows, incoming_half, preferred_element_type=jnp.float32
    )
    y_total = (y_inner + y_carry).reshape(row_count, inner_here) + jnp.repeat(skip_gain, head_size)[
        None, :
    ] * x_conv.astype(jnp.float32)
    gated = y_total * jax.nn.silu(gate_in.astype(jnp.float32))
    squares = lax.psum(jnp.sum(gated * gated, axis=1), "tp")
    square_mean = squares / (inner_here * lax.axis_size("tp"))
    normed = (gated * lax.rsqrt(square_mean + 1e-05)[:, None] * norm_gain).astype(jnp.bfloat16)
    partial_out = jnp.dot(
        normed,
        lax.all_gather(
            lax.all_gather(w_output, "sz", axis=1, tiled=True), "sx", axis=1, tiled=True
        ),
        preferred_element_type=jnp.float32,
    )
    summed = lax.psum_scatter(partial_out, "tp", scatter_dimension=1, tiled=True)
    live = in_block < jnp.repeat(local_valid, BLOCK)
    return jnp.where(live[:, None], summed, 0.0).astype(jnp.bfloat16)


def solution(mesh):
    seq_count, tp_count = mesh.devices.shape
    split = Mesh(
        mesh.devices.reshape(seq_count // SEQ_INNER, SEQ_INNER, tp_count), ("sx", "sz", "tp")
    )
    return jax.shard_map(
        on_device,
        mesh=split,
        in_specs=(
            P(SEQ, "tp"),
            P(SEQ, None, "tp"),
            P(SEQ, None),
            P(SEQ, "tp"),
            P(None, "tp"),
            P(),
            P("tp"),
            P("tp"),
            P("tp"),
            P("tp"),
            P("tp", SEQ),
            P(),
            P(),
        ),
        out_specs=P(SEQ, "tp"),
        check_vma=False,
    )
```

profile of v0, /device:TPU:1, one launch (start us, length us, event | category | flops | bytes accessed | tf_op | source)
XLA Modules:
  0.0 449.6 jit_solution(2950230188887680185)
XLA Ops:
  8.3 1.4 pad_maximum_fusion.4
  10.6 38.2 %all-gather.5.cloned.1.call-done = bf16[512,1288]{1,0:T(8,128)(2,1)} async-done(((bf16[64,1288]{1,0:T(8,128)(2,1)}), bf16[512,1288]{1,0:T(8,128)(2,1)}) %all-gather.5.cloned.1.call-update) | async-done | bytes 1318928 | tf_op jit(solution)/shard_map/all_gather | solution.py:74
  49.8 42.1 %all-gather.9.cloned.1.call-done = bf16[1024,2048]{1,0:T(8,128)(2,1)} async-done(((bf16[1024,256]{1,0:T(8,128)(2,1)}), bf16[1024,2048]{1,0:T(8,128)(2,1)}) %all-gather.9.cloned.1.call-update) | async-done | bytes 4194320 | tf_op jit(solution)/shard_map/all_gather | solution.py:68
  91.9 66.0 %all-gather.7.cloned.1.call-done = bf16[2048,1288]{1,0:T(8,128)(2,1)} async-done(((bf16[512,1288]{1,0:T(8,128)(2,1)}), bf16[2048,1288]{1,0:T(8,128)(2,1)}) %all-gather.7.cloned.1.call-update) | async-done | bytes 5275664 | tf_op jit(solution)/shard_map/all_gather | solution.py:73
  157.9 9.6 %fusion.10 = bf16[1024,1288]{0,1:T(8,128)(2,1)S(1)} fusion(bf16[2048,1288]{1,0:T(8,128)(2,1)} %all-gather.7.cloned.1.call-done, bf16[1024,2048]{1,0:T(8,128)(2,1)} %all-gather.9.cloned.1.call-done), kind=kOutput, calls=%fused_computation.20 | convolution fusion | flops 5403582464 | bytes 12107776 | tf_op jit(solution)/shard_map/dot_general | solution.py:76
  167.8 3.2 collective-permute-start
  171.0 3.2 collective-permute-start.1
  174.3 2.3 reduce-window.6
  177.8 2.3 slice.159
  183.5 1.8 maximum_convert_fusion
  185.3 3.1 multiply_convert_fusion.5
  188.4 2.6 reshape.134
  191.0 4.9 %fusion.15 = f32[4,8,128,64]{3,2,1,0:T(8,128)} fusion(f32[4,256,128]{2,1,0:T(8,128)} %copy.83, f32[4,256,8]{1,2,0:T(8,128)S(1)} %exponential_multiply_fusion, bf16[4,256,8,64]{1,0,3,2:T(4,128)(2,1)} %reshape.134), kind=kOutput, calls=%fused_computation.27 | convolution fusion | flops 136314880 | bytes 2654208 | tf_op jit(solution)/shard_map/cjhn,cjhp->chnp/dot_general | solution.py:107
  195.9 4.8 %while.26 = (s32[]{:T(128)}, f32[8]{0:T(128)S(1)}, f32[8,128,64]{2,1,0:T(8,128)S(1)}, f32[4,8]{1,0:T(4,128)S(1)}, f32[4,8,128,64]{3,2,1,0:T(8,128)}, /*index=5*/s32[]{:T(128)}, s32[]{:T(128)}) while((s32[]{:T(128)}, f32[8]{0:T(128)S(1)}, f32[8,128,64]{2,1,0:T(8,128)S(1)}, f32[4,8]{1,0:T(4,128)S(1)}, f32[4,8,128,64]{3,2,1,0:T(8,128)}, ...), condition=%wide.region_5.6_spmd.clone, body=%wide.region_4.5_spmd.clone.sunk | while | flops 196627 | bytes 786688 | solution.py:117
  201.1 3.2 collective-permute-start.2
  204.3 9.8 %collective-permute-done.2 = f32[8,129,64]{1,2,0:T(8,128)S(1)} collective-permute-done((f32[8,129,64]{1,2,0:T(8,128)S(1)}, f32[8,129,64]{1,2,0:T(8,128)S(1)}, u32[]{:S(2)}, u32[]{:S(2)}) %collective-permute-start.2) | collective-permute-done | bytes 264224 | tf_op jit(solution)/shard_map/ppermute | solution.py:16
  214.1 4.4 collective-permute-start.3
  218.7 8.8 %collective-permute-done.3 = f32[8,129,64]{1,2,0:T(8,128)S(1)} collective-permute-done((f32[8,129,64]{1,2,0:T(8,128)S(1)}, f32[8,129,64]{1,2,0:T(8,128)S(1)}, u32[]{:S(2)}, u32[]{:S(2)}) %collective-permute-start.3) | collective-permute-done | bytes 264224 | tf_op jit(solution)/shard_map/ppermute | solution.py:16
  227.7 6.1 %collective-permute-start.4 = (f32[8,129,64]{1,2,0:T(8,128)S(1)}, f32[8,129,64]{1,2,0:T(8,128)S(1)}, u32[]{:S(2)}, u32[]{:S(2)}) collective-permute-start(f32[8,129,64]{1,2,0:T(8,128)S(1)} %pad_maximum_fusion.1), channel_id=1, source_target_pairs={{0,16},{8,24},{16,32},{24,40},{32,48},{40,56},{48,64},{56,72},{64,... | collective-permute-start | bytes 792584 | tf_op jit(solution)/shard_map/ppermute | solution.py:16
  234.0 21.2 %collective-permute-done.4 = f32[8,129,64]{1,2,0:T(8,128)S(1)} collective-permute-done((f32[8,129,64]{1,2,0:T(8,128)S(1)}, f32[8,129,64]{1,2,0:T(8,128)S(1)}, u32[]{:S(2)}, u32[]{:S(2)}) %collective-permute-start.4) | collective-permute-done | bytes 264224 | tf_op jit(solution)/shard_map/ppermute | solution.py:16
  256.8 9.3 %collective-permute-start.5 = (f32[8,129,64]{1,2,0:T(8,128)}, f32[8,129,64]{1,2,0:T(8,128)}, u32[]{:S(2)}, u32[]{:S(2)}) collective-permute-start(f32[8,129,64]{1,2,0:T(8,128)} %pad_maximum_fusion.2), channel_id=1, source_target_pairs={{0,32},{8,40},{16,48},{24,56},{32,64},{40,72},{48,80},{56,88},{64,... | collective-permute-start | bytes 792584 | tf_op jit(solution)/shard_map/ppermute | solution.py:16
  266.1 40.6 %all_gather.18 = bf16[512,512]{0,1:T(8,128)(2,1)} all-gather(bf16[512,64]{0,1:T(8,128)(2,1)S(1)} %copy-done.6), channel_id=1, replica_groups=mesh['sx'=4,'sz'=8,'tp'=8] {'sz'}, dimensions={1}, use_global_device_ids=true | all-gather | bytes 589824 | tf_op jit(solution)/shard_map/all_gather | solution.py:161
  311.8 4.0 collective-permute-start.6
  315.8 1.3 fusion.37
  317.2 4.5 collective-permute-done.6
  322.0 20.4 %while.25 = (s32[]{:T(128)}, f32[8,128,64]{2,1,0:T(8,128)S(1)}, bf16[4,8,128,64]{3,2,1,0:T(8,128)(2,1)}, f32[4,8]{1,0:T(4,128)}, f32[4]{0:T(128)}, /*index=5*/f32[4,8,128,64]{3,2,1,0:T(8,128)}, s32[]{:T(128)}) while((s32[]{:T(128)}, f32[8,128,64]{2,1,0:T(8,128)S(1)}, bf16[4,8,128,64]{3,2,1,0:T(8,128)(2,1)}, f32[4,8]{1,0:T(4,128)}, ...), condition=%wide.region_7.8_spmd, body=%wide.region_6.7_spmd.sunk | while | flops 262146 | bytes 1574085 | solution.py:146
  322.0 1.2 dynamic_slice.45
  323.2 1.4 bitcast_dynamic-update-slice_fusion.2
  325.3 1.8 bitcast_add_fusion.5
  327.2 1.2 dynamic_slice.45
  328.4 1.4 bitcast_dynamic-update-slice_fusion.2
  330.4 1.8 bitcast_add_fusion.5
  332.3 1.2 dynamic_slice.45
  333.5 1.4 bitcast_dynamic-update-slice_fusion.2
  335.5 1.8 bitcast_add_fusion.5
  337.4 1.2 dynamic_slice.45
  338.6 1.4 bitcast_dynamic-update-slice_fusion.2
  340.7 1.8 bitcast_add_fusion.5
  342.5 2.4 copy.90
  344.9 1.6 fusion.63
  346.6 2.4 bitcast_add_fusion.2
  349.0 1.4 copy.91
  350.9 1.2 copy-done.2
  352.2 3.7 multiply_reduce_fusion
  355.9 29.0 %psum.7 = f32[1024]{0:T(1024)S(1)} all-reduce(f32[1024]{0:T(1024)S(1)} %get-tuple-element.165), channel_id=1, replica_groups=mesh['sx'=4,'sz'=8,'tp'=8] {'tp'}, use_global_device_ids=true, to_apply=%region_9.10 | all-reduce | flops 1024 | bytes 8192 | tf_op jit(solution)/shard_map/psum | solution.py:155
  384.9 7.9 %fusion.25 = f32[1024,2048]{0,1:T(8,128)} fusion(bf16[512,2048]{0,1:T(8,128)(2,1)} %all-gather.11.cloned.1.call-done, f32[1024,512]{0,1:T(8,128)} %get-tuple-element.166, f32[512]{0:T(512)S(1)} %copy-done.20, f32[1024]{0:T(1024)S(1)} %add_rsqrt_fusion), kind=kOutput, calls=%fused_computation.46 | convolution fusion | flops 2149056512 | bytes 12589056 | tf_op jit(solution)/shard_map/dot_general | solution.py:158
  393.8 47.0 %reduce-scatter.2.cloned.1.call-done = f32[1024,256]{0,1:T(8,128)} async-done(((f32[1024,2048]{0,1:T(8,128)}), f32[1024,256]{0,1:T(8,128)}) %reduce-scatter.2.cloned.1.call-update) | async-done | bytes 1048592 | tf_op jit(solution)/shard_map/reduce_scatter | solution.py:165
  440.8 1.3 select_convert_fusion
  (150 shorter events, 26.1 us)
Async XLA Ops:
  6.5 42.3 %copy-start.25 = (s32[128]{0:T(128)S(1)}, s32[128]{0:T(128)}, u32[]{:S(2)}) copy-start(s32[128]{0:T(128)} %param.28) | copy-start | bytes 1540
  6.5 43.0 %copy-start.24 = (f32[8]{0:T(128)S(1)}, f32[8]{0:T(128)}, u32[]{:S(2)}) copy-start(f32[8]{0:T(128)} %param.23) | copy-start | bytes 100
  6.5 43.1 %copy-start.19 = (f32[4,256]{1,0:T(4,128)S(1)}, f32[4,256]{1,0:T(4,128)}, u32[]{:S(2)}) copy-start(f32[4,256]{1,0:T(4,128)} %param.22) | copy-start | bytes 12292
  6.5 43.2 %copy-start.18 = (f32[4,512]{1,0:T(4,128)S(1)}, f32[4,512]{1,0:T(4,128)}, u32[]{:S(2)}) copy-start(f32[4,512]{1,0:T(4,128)} %param.21) | copy-start | bytes 24580
  6.5 42.2 %all-gather.5.cloned.1.call-start = ((), (), s32[]{:S(2)}) async-start(), calls=%async_computation.1 | async-start | bytes 1622016 | tf_op jit(solution)/shard_map/all_gather | solution.py:74
  9.8 82.1 %all-gather.9.cloned.1.call-start = ((), (), s32[]{:S(2)}) async-start(), calls=%async_computation.3 | async-start | bytes 4718592 | tf_op jit(solution)/shard_map/all_gather | solution.py:68
  10.5 147.4 %all-gather.7.cloned.1.call-start = ((), (), s32[]{:S(2)}) async-start(), calls=%async_computation.2 | async-start | bytes 7208960 | tf_op jit(solution)/shard_map/all_gather | solution.py:73
  48.8 336.2 %all-gather.11.cloned.1.call-start = ((), (), s32[]{:S(2)}) async-start(), calls=%async_computation.4 | async-start | bytes 2621440 | tf_op jit(solution)/shard_map/all_gather | solution.py:160
  49.0 0.5 copy-start.28
  49.7 128.1 %copy-start.22 = (f32[4]{0:T(128)}, f32[4]{0:T(128)S(1)}, u32[]{:S(2)}) copy-start(f32[4]{0:T(128)S(1)} %compare_select_fusion.1) | copy-start | bytes 52
  49.7 135.6 %copy-start.9 = (pred[1024]{0:T(1024)(128)(4,1)}, pred[1024]{0:T(1024)(128)(4,1)S(1)}, u32[]{:S(2)}) copy-start(pred[1024]{0:T(1024)(128)(4,1)S(1)} %get-tuple-element.181) | copy-start | bytes 3076
  49.7 135.6 %copy-start.11 = (pred[1024]{0:T(1024)(128)(4,1)}, pred[1024]{0:T(1024)(128)(4,1)S(1)}, u32[]{:S(2)}) copy-start(pred[1024]{0:T(1024)(128)(4,1)S(1)} %get-tuple-element.182) | copy-start | bytes 3076
  49.7 135.6 %copy-start.13 = (pred[1024]{0:T(1024)(128)(4,1)}, pred[1024]{0:T(1024)(128)(4,1)S(1)}, u32[]{:S(2)}) copy-start(pred[1024]{0:T(1024)(128)(4,1)S(1)} %get-tuple-element.183) | copy-start | bytes 3076
  49.7 135.6 %copy-start.15 = (pred[1024]{0:T(1024)(128)(4,1)}, pred[1024]{0:T(1024)(128)(4,1)S(1)}, u32[]{:S(2)}) copy-start(pred[1024]{0:T(1024)(128)(4,1)S(1)} %get-tuple-element.184) | copy-start | bytes 3076
  49.8 124.4 %copy-start.23 = (f32[8]{0:T(128)S(1)}, f32[8]{0:T(128)}, u32[]{:S(2)}) copy-start(f32[8]{0:T(128)} %param.24) | copy-start | bytes 100
  167.6 6.6 %copy-start.1 = (bf16[1024,1288]{0,1:T(8,128)(2,1)}, bf16[1024,1288]{0,1:T(8,128)(2,1)S(1)}, u32[]{:S(2)}) copy-start(bf16[1024,1288]{0,1:T(8,128)(2,1)S(1)} %fusion.10) | copy-start | bytes 7913476
  167.8 15.7 %collective-permute-start = (bf16[3,512]{0,1:T(8,128)(2,1)S(1)}, bf16[3,512]{0,1:T(8,128)(2,1)S(1)}, u32[]{:S(2)}, u32[]{:S(2)}) collective-permute-start(bf16[3,512]{0,1:T(8,128)(2,1)S(1)} %slice.158), channel_id=1, source_target_pairs={{0,8},{8,16},{16,24},{24,32},{32,40},{40,48},{48,56},{56,64},{64,7... | collective-permute-start | bytes 9224 | tf_op jit(solution)/shard_map/ppermute | solution.py:16
  171.0 9.1 %collective-permute-start.1 = (bf16[3,256]{0,1:T(8,128)(2,1)S(1)}, bf16[3,256]{0,1:T(8,128)(2,1)S(1)}, u32[]{:S(2)}, u32[]{:S(2)}) collective-permute-start(bf16[3,256]{0,1:T(8,128)(2,1)S(1)} %slice.167), channel_id=1, source_target_pairs={{0,8},{8,16},{16,24},{24,32},{32,40},{40,48},{48,56},{56,64},{64,7... | collective-permute-start | bytes 4616 | tf_op jit(solution)/shard_map/ppermute | solution.py:16
  174.3 5.8 %slice-start = ((bf16[1024,1288]{0,1:T(8,128)(2,1)}), bf16[1024,256]{0,1:T(8,128)(2,1)S(1)}, s32[]{:S(2)}) async-start(bf16[1024,1288]{0,1:T(8,128)(2,1)} %copy-done.1), calls=%async_computation.6 | async-start | bytes 1048576 | tf_op jit(solution)/shard_map/slice | solution.py:80
  177.7 2.7 copy-start.8
  201.1 13.0 %collective-permute-start.2 = (f32[8,129,64]{1,2,0:T(8,128)S(1)}, f32[8,129,64]{1,2,0:T(8,128)S(1)}, u32[]{:S(2)}, u32[]{:S(2)}) collective-permute-start(f32[8,129,64]{1,2,0:T(8,128)S(1)} %pad_maximum_fusion), channel_id=1, source_target_pairs={{0,8},{8,16},{16,24},{24,32},{32,40},{40,48},{48,56},{56,64},{64,7... | collective-permute-start | bytes 792584 | tf_op jit(solution)/shard_map/ppermute | solution.py:16
  214.1 13.4 %collective-permute-start.3 = (f32[8,129,64]{1,2,0:T(8,128)S(1)}, f32[8,129,64]{1,2,0:T(8,128)S(1)}, u32[]{:S(2)}, u32[]{:S(2)}) collective-permute-start(f32[8,129,64]{1,2,0:T(8,128)S(1)} %collective-permute-done.2), channel_id=1, source_target_pairs={{0,8},{8,16},{16,24},{24,32},{32,40},{40,48},{48,56},{56,64},{64,7... | collective-permute-start | bytes 792584 | tf_op jit(solution)/shard_map/ppermute | solution.py:16
  227.6 38.5 %copy-start.6 = (bf16[512,64]{0,1:T(8,128)(2,1)S(1)}, bf16[512,64]{0,1:T(8,128)(2,1)}, u32[]{:S(2)}) copy-start(bf16[512,64]{0,1:T(8,128)(2,1)} %param.27) | copy-start | bytes 196612
  227.7 79.2 %copy-start.21 = (f32[8]{0:T(128)S(1)}, f32[8]{0:T(128)}, u32[]{:S(2)}) copy-start(f32[8]{0:T(128)} %param.25) | copy-start | bytes 100
  227.7 27.5 %collective-permute-start.4 = (f32[8,129,64]{1,2,0:T(8,128)S(1)}, f32[8,129,64]{1,2,0:T(8,128)S(1)}, u32[]{:S(2)}, u32[]{:S(2)}) collective-permute-start(f32[8,129,64]{1,2,0:T(8,128)S(1)} %pad_maximum_fusion.1), channel_id=1, source_target_pairs={{0,16},{8,24},{16,32},{24,40},{32,48},{40,56},{48,64},{56,72},{64,... | collective-permute-start | bytes 792584 | tf_op jit(solution)/shard_map/ppermute | solution.py:16
  255.3 0.7 copy-start.4
  256.8 52.8 %collective-permute-start.5 = (f32[8,129,64]{1,2,0:T(8,128)}, f32[8,129,64]{1,2,0:T(8,128)}, u32[]{:S(2)}, u32[]{:S(2)}) collective-permute-start(f32[8,129,64]{1,2,0:T(8,128)} %pad_maximum_fusion.2), channel_id=1, source_target_pairs={{0,32},{8,40},{16,48},{24,56},{32,64},{40,72},{48,80},{56,88},{64,... | collective-permute-start | bytes 792584 | tf_op jit(solution)/shard_map/ppermute | solution.py:16
  306.8 134.0 %reduce-scatter.2.cloned.1.call-start = ((), (), s32[]{:S(2)}) async-start(), calls=%async_computation.5 | async-start | bytes 9437184 | tf_op jit(solution)/shard_map/reduce_scatter | solution.py:165
  308.7 13.1 %copy-start.3 = (bf16[1024,128]{1,0:T(8,128)(2,1)}, bf16[1024,128]{1,0:T(8,128)(2,1)S(1)}, u32[]{:S(2)}) copy-start(bf16[1024,128]{1,0:T(8,128)(2,1)S(1)} %copy.96) | copy-start | bytes 786436
  311.8 9.9 %collective-permute-start.6 = (f32[8,129,64]{1,2,0:T(8,128)S(1)}, f32[8,129,64]{1,2,0:T(8,128)S(1)}, u32[]{:S(2)}, u32[]{:S(2)}) collective-permute-start(f32[8,129,64]{1,2,0:T(8,128)S(1)} %pad_maximum_fusion.3), channel_id=1, source_target_pairs={{0,64},{8,72},{16,80},{24,88},{32,96},{40,104},{48,112},{56,120},{... | collective-permute-start | bytes 792584 | tf_op jit(solution)/shard_map/ppermute | solution.py:16
  342.5 4.1 copy-start
  344.9 1.7 copy-start.5
  344.9 1.7 copy-start.7
  350.4 1.7 copy-start.2
  350.4 1.7 copy-start.10
  350.4 1.7 copy-start.12
  350.4 1.7 copy-start.14
  350.4 1.7 copy-start.16
  350.4 1.7 copy-start.17
  352.2 32.8 %copy-start.20 = (f32[512]{0:T(512)S(1)}, f32[512]{0:T(512)}, u32[]{:S(2)}) copy-start(f32[512]{0:T(512)} %param.26) | copy-start | bytes 6148
  392.9 0.7 copy-start.26
  392.9 0.7 copy-start.27
  392.9 0.8 copy-start.29
Sparse Core Ops, SparseCore 0:
  9.9 38.8 all-gather.4
  50.6 41.3 all-gather.8
  93.7 64.1 all-gather.6
  306.9 37.4 all-gather.10
  393.0 47.7 reduce-scatter.1
where the time goes:
time: 451 us; the launch traced here: 450 us
  waiting for transfers between devices  238 us (53%)
  blocking collectives  69.7 us (15%)
  other arithmetic  37.5 us (8%)
  starting transfers between devices  33.5 us (7%)
  local copies, waits for them, and re-layouts  28.8 us (6%)
  matrix products  27.8 us (6%)
  between operations  13.8 us (3%)
    all_gather x1, waiting for transfers between devices, on_device(): lax.all_gather(lax.all_gather(joined, 'sz', axis=0, tiled=True), 'sx', ax...  66 us
    reduce_scatter x1, waiting for transfers between devices, on_device(): lax.psum_scatter(partial_out, 'tp', scatter_dimension=1, tiled=True)  47 us
    ppermute x7, waiting for transfers between devices, passed_along(): return lax.ppermute(value, axis, pairs)  44.4 us
    all_gather x1, waiting for transfers between devices, on_device(): whole = lax.all_gather(tokens, 'tp', axis=1, tiled=True)  42.1 us
    all_gather x1, blocking collectives, on_device(): lax.all_gather(w_output, 'sz', axis=1, tiled=True)  40.6 us
    all_gather x1, waiting for transfers between devices, on_device(): lax.all_gather(joined, 'sz', axis=0, tiled=True)  38.2 us
    ppermute x7, starting transfers between devices, passed_along(): return lax.ppermute(value, axis, pairs)  33.3 us
    psum x1, blocking collectives, on_device(): squares = lax.psum(jnp.sum(gated * gated, axis=1), 'tp')  29 us
  transfers between devices with their start and end apart: 12, of which 8 were waited for; matrix products, arithmetic and copies ran while one was open for 11% of the time, Pallas kernels for 0%

commit v1 on v0

--- a/solution.py
+++ b/solution.py
@@ -65,7 +65,28 @@
     local_valid = lax.dynamic_slice_in_dim(valid_rows, seq_index * local_blocks, local_blocks)
     in_block = jnp.arange(row_count, dtype=jnp.int32) % BLOCK
     carry_on = jnp.repeat(local_start == 0, BLOCK)
-    whole = lax.all_gather(tokens, "tp", axis=1, tiled=True)
+
+    def watch_slabs(local_x):
+        sheets = []
+        chips = lax.axis_size("tp")
+        for dd in range(chips):
+            sheets.append((dd, (dd + 1) % chips))
+        entries = []
+        for dd in range(chips):
+            entries.append((dd, (dd - 1) % chips))
+        b_next, r1 = ([local_x], [local_x])
+        for _ in range(chips // 2):
+            b_next.append(lax.ppermute(b_next[-1], "tp", sheets))
+        for _ in range((chips - 1) // 2):
+            r1.append(lax.ppermute(r1[-1], "tp", perm=entries))
+        val = jnp.roll(
+            jnp.concatenate([*b_next[::-1], *r1[1:]], axis=1),
+            shift=(lax.axis_index("tp") - chips // 2) * local_x.shape[1],
+            axis=1,
+        )
+        return val
+
+    whole = watch_slabs(tokens)
     local_rows = w_inner.shape[0]
     joined = jnp.concatenate(
         [w_inner.reshape(local_rows, 2 * inner_here), w_states, w_step], axis=1

time: 451 us -> 411 us (0.911)
  waiting for transfers between devices: 238 us -> 167 us
  starting transfers between devices: 33.5 us -> 50.5 us
  local copies, waits for them, and re-layouts: 28.8 us -> 43.2 us
    all_gather x1, waiting for transfers between devices: 66 us -> 16 us  [on_device(): lax.all_gather(lax.all_gather(joined, 'sz', axis=0, tiled=True), 'sx', ax...]
    all_gather x1 -> x0, waiting for transfers between devices: 42.1 us -> none  [on_device(): whole = lax.all_gather(tokens, 'tp', axis=1, tiled=True)]
    ppermute x0 -> x7, waiting for transfers between devices: none -> 20.6 us  [the longest x4 19.8 us: watch_slabs(): b_next.append(lax.ppermute(b_next[-1], 'tp', sheets))]
    ppermute x0 -> x7, starting transfers between devices: none -> 16.8 us  [the longest x4 13.5 us: watch_slabs(): b_next.append(lax.ppermute(b_next[-1], 'tp', sheets))]
    unnamed x65 -> x80, local copies, waits for them, and re-layouts: 5.18 us -> 18.7 us
  transfers between devices with their start and end apart: 12 -> 18, of which waited for: 8 -> 13; matrix products, arithmetic and copies ran while one was open for 11% -> 15% of each run, Pallas kernels for 0% -> 0%
where the time goes in v1:
time: 411 us; the launch traced here: 410 us
  waiting for transfers between devices  167 us (41%)
  blocking collectives  69.8 us (17%)
  starting transfers between devices  50.5 us (12%)
  local copies, waits for them, and re-layouts  43.2 us (11%)
  other arithmetic  38.6 us (9%)
  matrix products  26.3 us (6%)
  between operations  13.7 us (3%)
    reduce_scatter x1, waiting for transfers between devices, on_device(): lax.psum_scatter(partial_out, 'tp', scatter_dimension=1, tiled=True)  47.1 us
    ppermute x7, waiting for transfers between devices, passed_along(): return lax.ppermute(value, axis, pairs)  44.6 us
    all_gather x1, blocking collectives, on_device(): lax.all_gather(w_output, 'sz', axis=1, tiled=True)  40.4 us
    all_gather x1, waiting for transfers between devices, on_device(): lax.all_gather(joined, 'sz', axis=0, tiled=True)  38.9 us
    ppermute x7, starting transfers between devices, passed_along(): return lax.ppermute(value, axis, pairs)  33.3 us
    psum x1, blocking collectives, on_device(): squares = lax.psum(jnp.sum(gated * gated, axis=1), 'tp')  29.4 us
    ppermute x4, waiting for transfers between devices, watch_slabs(): b_next.append(lax.ppermute(b_next[-1], 'tp', sheets))  19.8 us
    unnamed x80, local copies, waits for them, and re-layouts  18.7 us
  transfers between devices with their start and end apart: 18, of which 13 were waited for; matrix products, arithmetic and copies ran while one was open for 15% of the time, Pallas kernels for 0%

profile of v1, /device:TPU:1, one launch (start us, length us, event | category | flops | bytes accessed | tf_op | source)
XLA Modules:
  0.0 409.6 jit_solution(5529282127130745406)
XLA Ops:
  8.3 1.4 pad_maximum_fusion.4
  9.9 38.9 %all-gather.4.cloned.1.call-done = bf16[512,1288]{1,0:T(8,128)(2,1)} async-done(((bf16[64,1288]{1,0:T(8,128)(2,1)}), bf16[512,1288]{1,0:T(8,128)(2,1)}) %all-gather.4.cloned.1.call-update) | async-done | bytes 1318928 | tf_op jit(solution)/shard_map/all_gather | solution.py:95
  48.9 6.1 %collective-permute-start = (bf16[1024,256]{1,0:T(8,128)(2,1)S(1)}, bf16[1024,256]{1,0:T(8,128)(2,1)S(1)}, u32[]{:S(2)}, u32[]{:S(2)}) collective-permute-start(bf16[1024,256]{1,0:T(8,128)(2,1)S(1)} %copy-done.2), channel_id=1, source_target_pairs={{0,1},{1,2},{2,3},{3,4},{4,5},{5,6},{6,7},{7,0},{8,9},{9,10},{10,1... | collective-permute-start | bytes 1572872 | tf_op jit(solution)/shard_map/ppermute | solution.py:79
  54.9 6.1 %collective-permute-done = bf16[1024,256]{1,0:T(8,128)(2,1)S(1)} collective-permute-done((bf16[1024,256]{1,0:T(8,128)(2,1)S(1)}, bf16[1024,256]{1,0:T(8,128)(2,1)S(1)}, u32[]{:S(2)}, u32[]{:S(2)}) %collective-permute-start) | collective-permute-done | bytes 524320 | tf_op jit(solution)/shard_map/ppermute | solution.py:79
  61.1 2.5 collective-permute-start.1
  63.9 5.8 %collective-permute-done.1 = bf16[1024,256]{1,0:T(8,128)(2,1)S(1)} collective-permute-done((bf16[1024,256]{1,0:T(8,128)(2,1)S(1)}, bf16[1024,256]{1,0:T(8,128)(2,1)S(1)}, u32[]{:S(2)}, u32[]{:S(2)}) %collective-permute-start.1) | collective-permute-done | bytes 524320 | tf_op jit(solution)/shard_map/ppermute | solution.py:79
  69.7 2.5 collective-permute-start.2
  73.8 4.5 %collective-permute-done.2 = bf16[1024,256]{1,0:T(8,128)(2,1)S(1)} collective-permute-done((bf16[1024,256]{1,0:T(8,128)(2,1)S(1)}, bf16[1024,256]{1,0:T(8,128)(2,1)S(1)}, u32[]{:S(2)}, u32[]{:S(2)}) %collective-permute-start.2) | collective-permute-done | bytes 524320 | tf_op jit(solution)/shard_map/ppermute | solution.py:79
  78.3 2.5 collective-permute-start.3
  81.6 2.0 collective-permute-start.6
  83.5 3.3 collective-permute-done.3
  101.1 16.0 %all-gather.6.cloned.1.call-done = bf16[2048,1288]{1,0:T(8,128)(2,1)} async-done(((bf16[512,1288]{1,0:T(8,128)(2,1)}), bf16[2048,1288]{1,0:T(8,128)(2,1)}) %all-gather.6.cloned.1.call-update) | async-done | bytes 5275664 | tf_op jit(solution)/shard_map/all_gather | solution.py:94
  117.1 9.3 %fusion.12 = bf16[1024,1288]{0,1:T(8,128)(2,1)S(1)} fusion(bf16[2048,1288]{1,0:T(8,128)(2,1)} %all-gather.6.cloned.1.call-done, bf16[1024,4096]{1,0:T(8,128)(2,1)} %constant_dynamic-update-slice_fusion, s32[]{:T(128)S(6)} %select_n.101), kind=kOutput, calls=%fused_computation.21 | convolution fusion | flops 5403582464 | bytes 12599300 | tf_op jit(solution)/shard_map/dot_general | solution.py:97
  128.0 3.2 collective-permute-start.8
  131.2 3.2 collective-permute-start.7
  134.5 2.3 reduce-window.6
  142.5 1.8 maximum_convert_fusion
  144.3 3.1 multiply_convert_fusion.5
  147.4 2.7 reshape.134
  150.0 4.9 %fusion.19 = f32[4,8,128,64]{3,2,1,0:T(8,128)} fusion(f32[4,256,128]{2,1,0:T(8,128)} %copy.83, f32[4,256,8]{1,2,0:T(8,128)S(1)} %exponential_multiply_fusion, bf16[4,256,8,64]{1,0,3,2:T(4,128)(2,1)} %reshape.134), kind=kOutput, calls=%fused_computation.28 | convolution fusion | flops 136314880 | bytes 2654208 | tf_op jit(solution)/shard_map/cjhn,cjhp->chnp/dot_general | solution.py:128
  155.0 4.8 %while.26 = (s32[]{:T(128)}, f32[8]{0:T(128)S(1)}, f32[8,128,64]{2,1,0:T(8,128)S(1)}, f32[4,8]{1,0:T(4,128)S(1)}, f32[4,8,128,64]{3,2,1,0:T(8,128)}, /*index=5*/s32[]{:T(128)}, s32[]{:T(128)}) while((s32[]{:T(128)}, f32[8]{0:T(128)S(1)}, f32[8,128,64]{2,1,0:T(8,128)S(1)}, f32[4,8]{1,0:T(4,128)S(1)}, f32[4,8,128,64]{3,2,1,0:T(8,128)}, ...), condition=%wide.region_5.6_spmd.clone, body=%wide.region_4.5_spmd.clone.sunk | while | flops 196627 | bytes 786688 | solution.py:138
  161.2 3.2 collective-permute-start.9
  164.5 9.8 %collective-permute-done.9 = f32[8,129,64]{1,2,0:T(8,128)S(1)} collective-permute-done((f32[8,129,64]{1,2,0:T(8,128)S(1)}, f32[8,129,64]{1,2,0:T(8,128)S(1)}, u32[]{:S(2)}, u32[]{:S(2)}) %collective-permute-start.9) | collective-permute-done | bytes 264224 | tf_op jit(solution)/shard_map/ppermute | solution.py:16
  174.3 4.4 %collective-permute-start.10 = (f32[8,129,64]{1,2,0:T(8,128)S(1)}, f32[8,129,64]{1,2,0:T(8,128)S(1)}, u32[]{:S(2)}, u32[]{:S(2)}) collective-permute-start(f32[8,129,64]{1,2,0:T(8,128)S(1)} %collective-permute-done.9), channel_id=1, source_target_pairs={{0,8},{8,16},{16,24},{24,32},{32,40},{40,48},{48,56},{56,64},{64,7... | collective-permute-start | bytes 792584 | tf_op jit(solution)/shard_map/ppermute | solution.py:16
  178.9 8.8 %collective-permute-done.10 = f32[8,129,64]{1,2,0:T(8,128)S(1)} collective-permute-done((f32[8,129,64]{1,2,0:T(8,128)S(1)}, f32[8,129,64]{1,2,0:T(8,128)S(1)}, u32[]{:S(2)}, u32[]{:S(2)}) %collective-permute-start.10) | collective-permute-done | bytes 264224 | tf_op jit(solution)/shard_map/ppermute | solution.py:16
  188.0 6.1 %collective-permute-start.11 = (f32[8,129,64]{1,2,0:T(8,128)S(1)}, f32[8,129,64]{1,2,0:T(8,128)S(1)}, u32[]{:S(2)}, u32[]{:S(2)}) collective-permute-start(f32[8,129,64]{1,2,0:T(8,128)S(1)} %pad_maximum_fusion.1), channel_id=1, source_target_pairs={{0,16},{8,24},{16,32},{24,40},{32,48},{40,56},{48,64},{56,72},{64,... | collective-permute-start | bytes 792584 | tf_op jit(solution)/shard_map/ppermute | solution.py:16
  194.2 21.3 %collective-permute-done.11 = f32[8,129,64]{1,2,0:T(8,128)S(1)} collective-permute-done((f32[8,129,64]{1,2,0:T(8,128)S(1)}, f32[8,129,64]{1,2,0:T(8,128)S(1)}, u32[]{:S(2)}, u32[]{:S(2)}) %collective-permute-start.11) | collective-permute-done | bytes 264224 | tf_op jit(solution)/shard_map/ppermute | solution.py:16
  217.1 9.3 %collective-permute-start.12 = (f32[8,129,64]{1,2,0:T(8,128)}, f32[8,129,64]{1,2,0:T(8,128)}, u32[]{:S(2)}, u32[]{:S(2)}) collective-permute-start(f32[8,129,64]{1,2,0:T(8,128)} %pad_maximum_fusion.2), channel_id=1, source_target_pairs={{0,32},{8,40},{16,48},{24,56},{32,64},{40,72},{48,80},{56,88},{64,... | collective-permute-start | bytes 792584 | tf_op jit(solution)/shard_map/ppermute | solution.py:16
  226.4 40.4 %all_gather.14 = bf16[512,512]{0,1:T(8,128)(2,1)} all-gather(bf16[512,64]{0,1:T(8,128)(2,1)S(1)} %copy-done.5), channel_id=1, replica_groups=mesh['sx'=4,'sz'=8,'tp'=8] {'sz'}, dimensions={1}, use_global_device_ids=true | all-gather | bytes 589824 | tf_op jit(solution)/shard_map/all_gather | solution.py:182
  272.0 4.0 collective-permute-start.13
  277.4 4.6 %collective-permute-done.13 = f32[8,129,64]{1,2,0:T(8,128)S(1)} collective-permute-done((f32[8,129,64]{1,2,0:T(8,128)S(1)}, f32[8,129,64]{1,2,0:T(8,128)S(1)}, u32[]{:S(2)}, u32[]{:S(2)}) %collective-permute-start.13) | collective-permute-done | bytes 264224 | tf_op jit(solution)/shard_map/ppermute | solution.py:16
  282.4 20.5 %while.25 = (s32[]{:T(128)}, f32[8,128,64]{2,1,0:T(8,128)S(1)}, bf16[4,8,128,64]{3,2,1,0:T(8,128)(2,1)}, f32[4,8]{1,0:T(4,128)}, f32[4]{0:T(128)}, /*index=5*/f32[4,8,128,64]{3,2,1,0:T(8,128)}, s32[]{:T(128)}) while((s32[]{:T(128)}, f32[8,128,64]{2,1,0:T(8,128)S(1)}, bf16[4,8,128,64]{3,2,1,0:T(8,128)(2,1)}, f32[4,8]{1,0:T(4,128)}, ...), condition=%wide.region_7.8_spmd, body=%wide.region_6.7_spmd.sunk | while | flops 262146 | bytes 1574085 | solution.py:167
  283.6 1.4 bitcast_dynamic-update-slice_fusion.2
  285.7 1.8 bitcast_add_fusion.5
  288.8 1.4 bitcast_dynamic-update-slice_fusion.2
  290.8 1.8 bitcast_add_fusion.5
  293.9 1.4 bitcast_dynamic-update-slice_fusion.2
  296.0 1.8 bitcast_add_fusion.5
  299.0 1.4 bitcast_dynamic-update-slice_fusion.2
  301.1 1.8 bitcast_add_fusion.5
  302.9 1.6 copy.90
  306.1 2.4 bitcast_add_fusion.2
  308.5 1.4 copy.91
  310.6 4.7 %multiply_reduce_fusion = (f32[1024]{0:T(1024)S(1)}, f32[1024,512]{0,1:T(8,128)}) fusion(bf16[1024,1288]{0,1:T(8,128)(2,1)} %copy-done.1, f32[1024,512]{0,1:T(8,128)S(1)} %bitcast.75, f32[512]{0:T(512)S(1)} %copy-done.17, f32[512]{0:T(512)S(1)} %bitcast.91, f32[1027,512]{0,1:T(8,128)S(1)} %maximum_convert_fusion, pred[1024]{0:T(1024)(128)(4,1)S(1)} %copy-done.12, ...), kind=kLoop, calls=%fused_computation.42 | loop fusion | flops 14154752 | bytes 13649920 | tf_op jit(solution)/shard_map/reduce_sum | solution.py:176
  315.3 29.4 %psum.7 = f32[1024]{0:T(1024)S(1)} all-reduce(f32[1024]{0:T(1024)S(1)} %get-tuple-element.165), channel_id=1, replica_groups=mesh['sx'=4,'sz'=8,'tp'=8] {'tp'}, use_global_device_ids=true, to_apply=%region_9.10 | all-reduce | flops 1024 | bytes 8192 | tf_op jit(solution)/shard_map/psum | solution.py:176
  344.8 7.9 %fusion.29 = f32[1024,2048]{0,1:T(8,128)} fusion(bf16[512,2048]{0,1:T(8,128)(2,1)} %all-gather.8.cloned.1.call-done, f32[1024,512]{0,1:T(8,128)} %get-tuple-element.166, f32[512]{0:T(512)S(1)} %copy-done.20, f32[1024]{0:T(1024)S(1)} %add_rsqrt_fusion), kind=kOutput, calls=%fused_computation.47 | convolution fusion | flops 2149056512 | bytes 12589056 | tf_op jit(solution)/shard_map/dot_general | solution.py:179
  353.6 47.1 %reduce-scatter.2.cloned.1.call-done = f32[1024,256]{0,1:T(8,128)} async-done(((f32[1024,2048]{0,1:T(8,128)}), f32[1024,256]{0,1:T(8,128)}) %reduce-scatter.2.cloned.1.call-update) | async-done | bytes 1048592 | tf_op jit(solution)/shard_map/reduce_scatter | solution.py:186
  400.7 1.3 select_convert_fusion
  (176 shorter events, 53.1 us)
Async XLA Ops:
  6.5 42.3 %copy-start.2 = (bf16[1024,256]{1,0:T(8,128)(2,1)S(1)}, bf16[1024,256]{1,0:T(8,128)(2,1)}, u32[]{:S(2)}) copy-start(bf16[1024,256]{1,0:T(8,128)(2,1)} %param.17) | copy-start | bytes 1572868
  6.5 57.1 %copy-start.25 = (s32[128]{0:T(128)S(1)}, s32[128]{0:T(128)}, u32[]{:S(2)}) copy-start(s32[128]{0:T(128)} %param.28) | copy-start | bytes 1540
  6.5 65.8 %copy-start.24 = (f32[8]{0:T(128)S(1)}, f32[8]{0:T(128)}, u32[]{:S(2)}) copy-start(f32[8]{0:T(128)} %param.23) | copy-start | bytes 100
  6.5 74.3 %copy-start.19 = (f32[4,256]{1,0:T(4,128)S(1)}, f32[4,256]{1,0:T(4,128)}, u32[]{:S(2)}) copy-start(f32[4,256]{1,0:T(4,128)} %param.22) | copy-start | bytes 12292
  6.5 74.3 %copy-start.18 = (f32[4,512]{1,0:T(4,128)S(1)}, f32[4,512]{1,0:T(4,128)}, u32[]{:S(2)}) copy-start(f32[4,512]{1,0:T(4,128)} %param.21) | copy-start | bytes 24580
  6.5 42.2 %all-gather.4.cloned.1.call-start = ((), (), s32[]{:S(2)}) async-start(), calls=%async_computation.1 | async-start | bytes 1622016 | tf_op jit(solution)/shard_map/all_gather | solution.py:95
  9.8 107.3 %all-gather.6.cloned.1.call-start = ((), (), s32[]{:S(2)}) async-start(), calls=%async_computation.2 | async-start | bytes 7208960 | tf_op jit(solution)/shard_map/all_gather | solution.py:94
  48.8 295.9 %all-gather.8.cloned.1.call-start = ((), (), s32[]{:S(2)}) async-start(), calls=%async_computation.3 | async-start | bytes 2621440 | tf_op jit(solution)/shard_map/all_gather | solution.py:181
  48.9 12.2 %collective-permute-start = (bf16[1024,256]{1,0:T(8,128)(2,1)S(1)}, bf16[1024,256]{1,0:T(8,128)(2,1)S(1)}, u32[]{:S(2)}, u32[]{:S(2)}) collective-permute-start(bf16[1024,256]{1,0:T(8,128)(2,1)S(1)} %copy-done.2), channel_id=1, source_target_pairs={{0,1},{1,2},{2,3},{3,4},{4,5},{5,6},{6,7},{7,0},{8,9},{9,10},{10,1... | collective-permute-start | bytes 1572872 | tf_op jit(solution)/shard_map/ppermute | solution.py:79
  61.1 8.6 %collective-permute-start.1 = (bf16[1024,256]{1,0:T(8,128)(2,1)S(1)}, bf16[1024,256]{1,0:T(8,128)(2,1)S(1)}, u32[]{:S(2)}, u32[]{:S(2)}) collective-permute-start(bf16[1024,256]{1,0:T(8,128)(2,1)S(1)} %collective-permute-done), channel_id=1, source_target_pairs={{0,1},{1,2},{2,3},{3,4},{4,5},{5,6},{6,7},{7,0},{8,9},{9,10},{10,1... | collective-permute-start | bytes 1572872 | tf_op jit(solution)/shard_map/ppermute | solution.py:79
  63.6 9.0 %collective-permute-start.4 = (bf16[1024,256]{1,0:T(8,128)(2,1)S(1)}, bf16[1024,256]{1,0:T(8,128)(2,1)S(1)}, u32[]{:S(2)}, u32[]{:S(2)}) collective-permute-start(bf16[1024,256]{1,0:T(8,128)(2,1)S(1)} %copy-done.2), channel_id=1, source_target_pairs={{0,7},{1,0},{2,1},{3,2},{4,3},{5,4},{6,5},{7,6},{8,15},{9,8},{10,9... | collective-permute-start | bytes 1572872 | tf_op jit(solution)/shard_map/ppermute | solution.py:81
  63.9 8.4 %copy-start.28 = (s32[128]{0:T(128)}, s32[128]{0:T(128)S(1)}, u32[]{:S(2)}) copy-start(s32[128]{0:T(128)S(1)} %select_reduce_fusion) | copy-start | bytes 1540
  69.7 8.6 %collective-permute-start.2 = (bf16[1024,256]{1,0:T(8,128)(2,1)S(1)}, bf16[1024,256]{1,0:T(8,128)(2,1)S(1)}, u32[]{:S(2)}, u32[]{:S(2)}) collective-permute-start(bf16[1024,256]{1,0:T(8,128)(2,1)S(1)} %collective-permute-done.1), channel_id=1, source_target_pairs={{0,1},{1,2},{2,3},{3,4},{4,5},{5,6},{6,7},{7,0},{8,9},{9,10},{10,1... | collective-permute-start | bytes 1572872 | tf_op jit(solution)/shard_map/ppermute | solution.py:79
  72.4 71.9 %copy-start.9 = (pred[1024]{0:T(1024)(128)(4,1)}, pred[1024]{0:T(1024)(128)(4,1)S(1)}, u32[]{:S(2)}) copy-start(pred[1024]{0:T(1024)(128)(4,1)S(1)} %get-tuple-element.181) | copy-start | bytes 3076
  72.4 71.9 %copy-start.11 = (pred[1024]{0:T(1024)(128)(4,1)}, pred[1024]{0:T(1024)(128)(4,1)S(1)}, u32[]{:S(2)}) copy-start(pred[1024]{0:T(1024)(128)(4,1)S(1)} %get-tuple-element.182) | copy-start | bytes 3076
  72.4 71.9 %copy-start.13 = (pred[1024]{0:T(1024)(128)(4,1)}, pred[1024]{0:T(1024)(128)(4,1)S(1)}, u32[]{:S(2)}) copy-start(pred[1024]{0:T(1024)(128)(4,1)S(1)} %get-tuple-element.183) | copy-start | bytes 3076
  72.4 71.9 %copy-start.15 = (pred[1024]{0:T(1024)(128)(4,1)}, pred[1024]{0:T(1024)(128)(4,1)S(1)}, u32[]{:S(2)}) copy-start(pred[1024]{0:T(1024)(128)(4,1)S(1)} %get-tuple-element.184) | copy-start | bytes 3076
  72.6 9.0 %collective-permute-start.5 = (bf16[1024,256]{1,0:T(8,128)(2,1)S(1)}, bf16[1024,256]{1,0:T(8,128)(2,1)S(1)}, u32[]{:S(2)}, u32[]{:S(2)}) collective-permute-start(bf16[1024,256]{1,0:T(8,128)(2,1)S(1)} %collective-permute-done.4), channel_id=1, source_target_pairs={{0,7},{1,0},{2,1},{3,2},{4,3},{5,4},{6,5},{7,6},{8,15},{9,8},{10,9... | collective-permute-start | bytes 1572872 | tf_op jit(solution)/shard_map/ppermute | solution.py:81
  78.3 8.6 %collective-permute-start.3 = (bf16[1024,256]{1,0:T(8,128)(2,1)S(1)}, bf16[1024,256]{1,0:T(8,128)(2,1)S(1)}, u32[]{:S(2)}, u32[]{:S(2)}) collective-permute-start(bf16[1024,256]{1,0:T(8,128)(2,1)S(1)} %collective-permute-done.2), channel_id=1, source_target_pairs={{0,1},{1,2},{2,3},{3,4},{4,5},{5,6},{6,7},{7,0},{8,9},{9,10},{10,1... | collective-permute-start | bytes 1572872 | tf_op jit(solution)/shard_map/ppermute | solution.py:79
  80.8 57.1 %copy-start.22 = (f32[4]{0:T(128)}, f32[4]{0:T(128)S(1)}, u32[]{:S(2)}) copy-start(f32[4]{0:T(128)S(1)} %compare_select_fusion.1) | copy-start | bytes 52
  81.6 11.5 %collective-permute-start.6 = (bf16[1024,256]{1,0:T(8,128)(2,1)S(1)}, bf16[1024,256]{1,0:T(8,128)(2,1)S(1)}, u32[]{:S(2)}, u32[]{:S(2)}) collective-permute-start(bf16[1024,256]{1,0:T(8,128)(2,1)S(1)} %collective-permute-done.5), channel_id=1, source_target_pairs={{0,7},{1,0},{2,1},{3,2},{4,3},{5,4},{6,5},{7,6},{8,15},{9,8},{10,9... | collective-permute-start | bytes 1572872 | tf_op jit(solution)/shard_map/ppermute | solution.py:81
  101.1 33.3 %copy-start.23 = (f32[8]{0:T(128)S(1)}, f32[8]{0:T(128)}, u32[]{:S(2)}) copy-start(f32[8]{0:T(128)} %param.24) | copy-start | bytes 100
  126.4 12.9 %copy-start.1 = (bf16[1024,1288]{0,1:T(8,128)(2,1)}, bf16[1024,1288]{0,1:T(8,128)(2,1)S(1)}, u32[]{:S(2)}) copy-start(bf16[1024,1288]{0,1:T(8,128)(2,1)S(1)} %fusion.12) | copy-start | bytes 7913476
  128.0 11.1 %collective-permute-start.8 = (bf16[3,256]{0,1:T(8,128)(2,1)}, bf16[3,256]{0,1:T(8,128)(2,1)S(1)}, u32[]{:S(2)}, u32[]{:S(2)}) collective-permute-start(bf16[3,256]{0,1:T(8,128)(2,1)} %slice.167), channel_id=1, source_target_pairs={{0,8},{8,16},{16,24},{24,32},{32,40},{40,48},{48,56},{56,64},{64,7... | collective-permute-start | bytes 4616 | tf_op jit(solution)/shard_map/ppermute | solution.py:16
  131.2 11.3 %collective-permute-start.7 = (bf16[3,512]{0,1:T(8,128)(2,1)}, bf16[3,512]{0,1:T(8,128)(2,1)S(1)}, u32[]{:S(2)}, u32[]{:S(2)}) collective-permute-start(bf16[3,512]{0,1:T(8,128)(2,1)} %slice.158), channel_id=1, source_target_pairs={{0,8},{8,16},{16,24},{24,32},{32,40},{40,48},{48,56},{56,64},{64,7... | collective-permute-start | bytes 9224 | tf_op jit(solution)/shard_map/ppermute | solution.py:16
  137.8 1.5 copy-start.8
  159.7 0.5 copy-start.7
  161.2 13.1 %collective-permute-start.9 = (f32[8,129,64]{1,2,0:T(8,128)S(1)}, f32[8,129,64]{1,2,0:T(8,128)S(1)}, u32[]{:S(2)}, u32[]{:S(2)}) collective-permute-start(f32[8,129,64]{1,2,0:T(8,128)S(1)} %pad_maximum_fusion), channel_id=1, source_target_pairs={{0,8},{8,16},{16,24},{24,32},{32,40},{40,48},{48,56},{56,64},{64,7... | collective-permute-start | bytes 792584 | tf_op jit(solution)/shard_map/ppermute | solution.py:16
  174.3 13.4 %collective-permute-start.10 = (f32[8,129,64]{1,2,0:T(8,128)S(1)}, f32[8,129,64]{1,2,0:T(8,128)S(1)}, u32[]{:S(2)}, u32[]{:S(2)}) collective-permute-start(f32[8,129,64]{1,2,0:T(8,128)S(1)} %collective-permute-done.9), channel_id=1, source_target_pairs={{0,8},{8,16},{16,24},{24,32},{32,40},{40,48},{48,56},{56,64},{64,7... | collective-permute-start | bytes 792584 | tf_op jit(solution)/shard_map/ppermute | solution.py:16
  187.8 38.6 %copy-start.5 = (bf16[512,64]{0,1:T(8,128)(2,1)S(1)}, bf16[512,64]{0,1:T(8,128)(2,1)}, u32[]{:S(2)}) copy-start(bf16[512,64]{0,1:T(8,128)(2,1)} %param.27) | copy-start | bytes 196612
  187.9 79.2 %copy-start.21 = (f32[8]{0:T(128)S(1)}, f32[8]{0:T(128)}, u32[]{:S(2)}) copy-start(f32[8]{0:T(128)} %param.25) | copy-start | bytes 100
  188.0 27.5 %collective-permute-start.11 = (f32[8,129,64]{1,2,0:T(8,128)S(1)}, f32[8,129,64]{1,2,0:T(8,128)S(1)}, u32[]{:S(2)}, u32[]{:S(2)}) collective-permute-start(f32[8,129,64]{1,2,0:T(8,128)S(1)} %pad_maximum_fusion.1), channel_id=1, source_target_pairs={{0,16},{8,24},{16,32},{24,40},{32,48},{40,56},{48,64},{56,72},{64,... | collective-permute-start | bytes 792584 | tf_op jit(solution)/shard_map/ppermute | solution.py:16
  215.5 0.7 copy-start.3
  217.1 52.8 %collective-permute-start.12 = (f32[8,129,64]{1,2,0:T(8,128)}, f32[8,129,64]{1,2,0:T(8,128)}, u32[]{:S(2)}, u32[]{:S(2)}) collective-permute-start(f32[8,129,64]{1,2,0:T(8,128)} %pad_maximum_fusion.2), channel_id=1, source_target_pairs={{0,32},{8,40},{16,48},{24,56},{32,64},{40,72},{48,80},{56,88},{64,... | collective-permute-start | bytes 792584 | tf_op jit(solution)/shard_map/ppermute | solution.py:16
  266.8 133.9 %reduce-scatter.2.cloned.1.call-start = ((), (), s32[]{:S(2)}) async-start(), calls=%async_computation.4 | async-start | bytes 9437184 | tf_op jit(solution)/shard_map/reduce_scatter | solution.py:186
  272.0 10.0 %collective-permute-start.13 = (f32[8,129,64]{1,2,0:T(8,128)S(1)}, f32[8,129,64]{1,2,0:T(8,128)S(1)}, u32[]{:S(2)}, u32[]{:S(2)}) collective-permute-start(f32[8,129,64]{1,2,0:T(8,128)S(1)} %pad_maximum_fusion.3), channel_id=1, source_target_pairs={{0,64},{8,72},{16,80},{24,88},{32,96},{40,104},{48,112},{56,120},{... | collective-permute-start | bytes 792584 | tf_op jit(solution)/shard_map/ppermute | solution.py:16
  302.9 2.1 copy-start.6
  304.5 1.2 copy-start
  304.6 1.5 copy-start.4
  309.9 0.7 copy-start.10
  309.9 0.7 copy-start.12
  309.9 0.7 copy-start.14
  309.9 0.7 copy-start.16
  309.9 0.7 copy-start.17
  310.6 34.2 %copy-start.20 = (f32[512]{0:T(512)S(1)}, f32[512]{0:T(512)}, u32[]{:S(2)}) copy-start(f32[512]{0:T(512)} %param.26) | copy-start | bytes 6148
  352.7 0.7 copy-start.26
  352.7 0.7 copy-start.27
  352.7 0.8 copy-start.29
Sparse Core Ops, SparseCore 0:
  9.9 38.8 all-gather.3
  50.6 66.4 all-gather.5
  267.0 37.6 all-gather.7
  352.9 47.8 reduce-scatter.1
